TPU v7x, 128 devices: a whole 4x4x4 slice. The times are simulated.
128 devices in a mesh: row: 16 (over z, x), col: 8 (over y, core).
Axes of the slice: x: 4, y: 4, z: 4, core: 2. Of those that a mesh axis runs over, the one named last changes fastest.
Arguments:
- inputs: bfloat16 [2048, 6144], P('col', 'row'), may hold values from -6 to 6
- out_grad: bfloat16 [2048, 6144], P('col', 'row'), may hold values from -6 to 6
- pre_act: bfloat16 [2048, 24576], P('row', 'col'), may hold values from -8 to 8
- w_in: bfloat16 [6144, 24576], P('row', 'col'), may hold values from -0.078125 to 0.078125
- w_out: bfloat16 [24576, 6144], P('col', 'row'), may hold values from -0.0390625 to 0.0390625
Outputs:
- in_grad: bfloat16 [2048, 6144], P('col', 'row')
- w_in_grad: bfloat16 [6144, 24576], P('row', 'col')
- w_out_grad: bfloat16 [24576, 6144], P('col', 'row')
All inputs are finite; a program needn't handle non-finite values.
Results may differ from a plain program's by a relative error of at most 0.03.
Values may be sent and summed in bfloat16 or wider, within the bound.
No kernel may reach another device: no remote copies, remote signals or barrier semaphores. Data moves between devices by JAX's collectives and lax.ppermute only.
A program may use at most 128 MiB of HBM per device.

v0:
```python
import jax
import jax.numpy as jnp
from jax import lax
from jax.sharding import PartitionSpec as P


def gelu_parts(pre_act):
    value = pre_act.astype(jnp.float32)
    cumul = 0.5 * (1.0 + jax.scipy.special.erf(value * 0.7071067811865476))
    density = jnp.exp(-0.5 * value * value) * 0.3989422804014327
    return (value * cumul, cumul + value * density)


def on_device(inputs, out_grad, pre_act, w_in, w_out):
    inputs_all, grad_all = (
        lax.all_gather(inputs, "col", axis=0, tiled=True),
        lax.all_gather(out_grad, "col", axis=0, tiled=True),
    )
    block = grad_all
    total = lax.psum(
        lax.dot_general(
            block, w_out, (((1,), (1,)), ((), ())), preferred_element_type=jnp.float32
        ).astype(jnp.bfloat16),
        "row",
    ).astype(jnp.float32)
    pre_all = lax.all_gather(pre_act, "row", axis=0, tiled=True)
    value, slope = gelu_parts(pre_all)
    hidden = value.astype(jnp.bfloat16)
    pre_grad = (total * slope).astype(jnp.bfloat16)
    w_out_grad = lax.dot_general(
        hidden, grad_all, (((0,), (0,)), ((), ())), preferred_element_type=jnp.float32
    ).astype(jnp.bfloat16)
    w_in_grad = lax.dot_general(
        inputs_all, pre_grad, (((0,), (0,)), ((), ())), preferred_element_type=jnp.float32
    ).astype(jnp.bfloat16)
    block = pre_grad
    in_grad = lax.psum_scatter(
        lax.dot_general(
            block, w_in, (((1,), (1,)), ((), ())), preferred_element_type=jnp.float32
        ).astype(jnp.bfloat16),
        "col",
        scatter_dimension=0,
        tiled=True,
    )
    return (in_grad, w_in_grad, w_out_grad)


def solution(mesh):
    in_specs = (P("col", "row"), P("col", "row"), P("row", "col"), P("row", "col"), P("col", "row"))
    out_specs = (P("col", "row"), P("row", "col"), P("col", "row"))
    return jax.shard_map(
        on_device, mesh=mesh, in_specs=in_specs, out_specs=out_specs, check_vma=False
    )
```

profile of v0, /device:TPU:0, one launch (start us, length us, event | category | flops | bytes accessed | tf_op | source)
XLA Modules:
  0.0 386.3 jit_solution(935208402461848215)
XLA Ops:
  7.2 0.0 copy-start
  7.2 0.0 all-gather.4.cloned.1.call-start
  7.2 0.7 all-gather.4.cloned.1.call-update
  7.9 0.0 all-reduce.2.cloned.1.call-start
  8.0 28.5 %all-gather.4.cloned.1.call-done = bf16[2048,384]{1,0:T(8,128)(2,1)} async-done(((bf16[256,384]{1,0:T(8,128)(2,1)}), bf16[2048,384]{1,0:T(8,128)(2,1)}) %all-gather.4.cloned.1.call-update) | async-done | bytes 1572880 | tf_op jit(solution)/shard_map/all_gather | solution.py:17
  36.5 11.2 %convolution_convert_fusion = bf16[2048,3072]{1,0:T(8,128)(2,1)} fusion(bf16[2048,384]{1,0:T(8,128)(2,1)} %all-gather.4.cloned.1.call-done, bf16[3072,384]{1,0:T(8,128)(2,1)S(1)} %copy-done), kind=kOutput, calls=%fused_computation.15 | convolution fusion | flops 4838129664 | bytes 16515072 | tf_op jit(solution)/shard_map/dot_general | solution.py:21
  47.6 0.0 all-reduce.2.cloned.1.call-update
  47.7 0.0 all-gather.6.cloned.1.call-start
  47.7 0.7 all-gather.6.cloned.1.call-update
  48.4 0.0 all-gather.8.cloned.1.call-start
  48.5 0.5 all-gather.8.cloned.1.call-update
  49.0 0.0 copy-start.3
  49.0 0.0 reduce-scatter.2.cloned.1.call-start
  49.0 177.4 %all-reduce.2.cloned.1.call-done = bf16[2048,3072]{1,0:T(8,128)(2,1)} async-done(((bf16[2048,3072]{1,0:T(8,128)(2,1)}), bf16[2048,3072]{1,0:T(8,128)(2,1)}) %all-reduce.2.cloned.1.call-update) | async-done | bytes 12582928 | tf_op jit(solution)/shard_map/psum | solution.py:20
  226.4 91.8 %all-gather.6.cloned.1.call-done = bf16[2048,3072]{1,0:T(8,128)(2,1)} async-done(((bf16[128,3072]{1,0:T(8,128)(2,1)}), bf16[2048,3072]{1,0:T(8,128)(2,1)}) %all-gather.6.cloned.1.call-update) | async-done | bytes 12582928 | tf_op jit(solution)/shard_map/all_gather | solution.py:26
  318.2 13.7 %fusion.7 = bf16[2048,3072]{1,0:T(8,128)(2,1)S(1)} fusion(bf16[2048,3072]{1,0:T(8,128)(2,1)} %all-gather.6.cloned.1.call-done, bf16[2048,3072]{1,0:T(8,128)(2,1)} %all-reduce.2.cloned.1.call-done), kind=kLoop, calls=%fused_computation.12 | loop fusion | flops 75497472 | bytes 37748736 | tf_op jit(solution)/shard_map/convert_element_type | solution.py:29
  331.9 4.5 %copy-done.2 = bf16[2048,3072]{1,0:T(8,128)(2,1)} copy-done((bf16[2048,3072]{1,0:T(8,128)(2,1)}, bf16[2048,3072]{1,0:T(8,128)(2,1)S(1)}, u32[]{:S(2)}) %copy-start.2) | copy-done | bytes 12582936
  336.4 7.8 %convolution_convert_fusion.2 = bf16[2048,384]{1,0:T(8,128)(2,1)} fusion(bf16[2048,3072]{1,0:T(8,128)(2,1)S(1)} %fusion.7, bf16[384,3072]{1,0:T(8,128)(2,1)S(1)} %copy-done.3), kind=kOutput, calls=%fused_computation.19 | convolution fusion | flops 4832624640 | bytes 16515072 | tf_op jit(solution)/shard_map/dot_general | solution.py:38
  344.2 0.0 reduce-scatter.2.cloned.1.call-update
  344.2 0.0 all-gather.8.cloned.1.call-done
  344.2 10.2 %fusion.14 = bf16[384,3072]{0,1:T(8,128)(2,1)S(1)} fusion(bf16[2048,3072]{1,0:T(8,128)(2,1)} %copy-done.2, bf16[2048,384]{1,0:T(8,128)(2,1)} %all-gather.8.cloned.1.call-done), kind=kOutput, calls=%fused_computation.18 | convolution fusion | flops 4833017856 | bytes 16515072 | tf_op jit(solution)/shard_map/dot_general | solution.py:33
  354.4 2.6 copy.8
  357.0 11.9 %fusion.11 = bf16[3072,384]{1,0:T(8,128)(2,1)} fusion(bf16[2048,384]{1,0:T(8,128)(2,1)} %all-gather.4.cloned.1.call-done, bf16[2048,3072]{1,0:T(8,128)(2,1)} %all-gather.6.cloned.1.call-done), kind=kOutput, calls=%fused_computation.16 | convolution fusion | flops 4870766592 | bytes 16515072 | tf_op jit(solution)/shard_map/dot_general | solution.py:30
  368.9 10.8 %reduce-scatter.2.cloned.1.call-done = bf16[256,384]{1,0:T(8,128)(2,1)} async-done(((bf16[2048,384]{1,0:T(8,128)(2,1)}), bf16[256,384]{1,0:T(8,128)(2,1)}) %reduce-scatter.2.cloned.1.call-update) | async-done | bytes 196624 | tf_op jit(solution)/shard_map/reduce_scatter | solution.py:37
  (5 shorter events, 0.0 us)
Async XLA Ops:
  7.2 29.3 %copy-start = (bf16[3072,384]{1,0:T(8,128)(2,1)S(1)}, bf16[3072,384]{1,0:T(8,128)(2,1)}, u32[]{:S(2)}) copy-start(bf16[3072,384]{1,0:T(8,128)(2,1)} %param.9) | copy-start | bytes 7077892
  7.2 29.3 %all-gather.4.cloned.1.call-start = ((), (), s32[]{:S(2)}) async-start(), calls=%async_computation.1 | async-start | bytes 1769472 | tf_op jit(solution)/shard_map/all_gather | solution.py:17
  7.9 218.5 %all-reduce.2.cloned.1.call-start = ((), (), s32[]{:S(2)}) async-start(), calls=%async_computation.2 | async-start | bytes 25165824 | tf_op jit(solution)/shard_map/psum | solution.py:20
  47.7 270.5 %all-gather.6.cloned.1.call-start = ((), (), s32[]{:S(2)}) async-start(), calls=%async_computation.3 | async-start | bytes 13369344 | tf_op jit(solution)/shard_map/all_gather | solution.py:26
  48.4 295.8 %all-gather.8.cloned.1.call-start = ((), (), s32[]{:S(2)}) async-start(), calls=%async_computation.5 | async-start | bytes 1769472 | tf_op jit(solution)/shard_map/all_gather | solution.py:16
  49.0 287.4 %copy-start.3 = (bf16[384,3072]{1,0:T(8,128)(2,1)S(1)}, bf16[384,3072]{1,0:T(8,128)(2,1)}, u32[]{:S(2)}) copy-start(bf16[384,3072]{1,0:T(8,128)(2,1)} %param.8) | copy-start | bytes 7077892
  49.0 330.7 %reduce-scatter.2.cloned.1.call-start = ((), (), s32[]{:S(2)}) async-start(), calls=%async_computation.4 | async-start | bytes 1769472 | tf_op jit(solution)/shard_map/reduce_scatter | solution.py:37
  331.9 4.5 %copy-start.2 = (bf16[2048,3072]{1,0:T(8,128)(2,1)}, bf16[2048,3072]{1,0:T(8,128)(2,1)S(1)}, u32[]{:S(2)}) copy-start(bf16[2048,3072]{1,0:T(8,128)(2,1)S(1)} %fusion.7) | copy-start | bytes 37748740
  357.0 22.7 %copy-start.1 = (bf16[3072,384]{1,0:T(8,128)(2,1)S(1)}, bf16[3072,384]{1,0:T(8,128)(2,1)}, u32[]{:S(2)}) copy-start(bf16[3072,384]{1,0:T(8,128)(2,1)} %param.9) | copy-start | bytes 7077892
Sparse Core Ops, SparseCore 0:
  9.7 26.7 all-gather.3
  47.8 178.6 all-reduce.1
  228.6 89.5 all-gather.5
  319.8 23.8 all-gather.7
  346.5 33.1 reduce-scatter.1
where the time goes:
time: 387 us; the launch traced here: 386 us
  waiting for transfers between devices  310 us (80%)
  matrix products  41 us (11%)
  between operations  13.8 us (4%)
  other arithmetic  13.7 us (4%)
  local copies, waits for them, and re-layouts  7.09 us (2%)
    psum x1, waiting for transfers between devices, on_device(): lax.psum(lax.dot_general(block, w_out, (((1,), (1,)), ((), ())), preferre...  177 us
    all_gather x1, waiting for transfers between devices, on_device(): pre_all = lax.all_gather(pre_act, 'row', axis=0, tiled=True)  91.8 us
    all_gather x1, waiting for transfers between devices, on_device(): lax.all_gather(out_grad, 'col', axis=0, tiled=True)  28.5 us
    convert_element_type x1, other arithmetic, on_device(): pre_grad = (total * slope).astype(jnp.bfloat16)  13.7 us
    dot_general x1, matrix products, on_device(): lax.dot_general(hidden, grad_all, (((0,), (0,)), ((), ())), preferred_ele...  11.9 us
    dot_general x1, matrix products, on_device(): lax.dot_general(block, w_out, (((1,), (1,)), ((), ())), preferred_element...  11.2 us
    reduce_scatter x1, waiting for transfers between devices, on_device(): lax.psum_scatter(lax.dot_general(block, w_in, (((1,), (1,)), ((), ())), p...  10.8 us
    dot_general x1, matrix products, on_device(): lax.dot_general(inputs_all, pre_grad, (((0,), (0,)), ((), ())), preferred...  10.2 us
  transfers between devices with their start and end apart: 5, of which 4 were waited for; matrix products, arithmetic and copies ran while one was open for 12% of the time, Pallas kernels for 0%

commit v1 on v0

--- a/solution.py
+++ b/solution.py
@@ -2,6 +2,18 @@
 import jax.numpy as jnp
 from jax import lax
 from jax.sharding import PartitionSpec as P
+
+
+def launch_the_shelves(page, mesh_dim="row"):
+    count_all = lax.axis_size(mesh_dim)
+    block_last = lax.all_to_all(
+        jnp.tile(page, [count_all if it == 0 else 1 for it in range(page.ndim)]),
+        mesh_dim,
+        split_axis=0,
+        concat_axis=0,
+        tiled=True,
+    )
+    return block_last
 
 
 def gelu_parts(pre_act):
@@ -23,7 +35,7 @@
         ).astype(jnp.bfloat16),
         "row",
     ).astype(jnp.float32)
-    pre_all = lax.all_gather(pre_act, "row", axis=0, tiled=True)
+    pre_all = launch_the_shelves(pre_act)
     value, slope = gelu_parts(pre_all)
     hidden = value.astype(jnp.bfloat16)
     pre_grad = (total * slope).astype(jnp.bfloat16)

time: 387 us -> 463 us (1.20)
  waiting for transfers between devices: 310 us -> 361 us
  local copies, waits for them, and re-layouts: 7.09 us -> 14.3 us
  starting transfers between devices: 0.19 us -> 7.32 us
  matrix products: 41 us -> 46.6 us
  other arithmetic: 13.7 us -> 19.3 us
    all_to_all x0 -> x1, waiting for transfers between devices: none -> 217 us  [launch_the_shelves(): lax.all_to_all(jnp.tile(page, [count_all if it == 0 else 1 for it in rang...]
    all_gather x1 -> x0, waiting for transfers between devices: 91.8 us -> none  [on_device(): pre_all = lax.all_gather(pre_act, 'row', axis=0, tiled=True)]
    psum x1, waiting for transfers between devices: 177 us -> 112 us  [on_device(): lax.psum(lax.dot_general(block, w_out, (((1,), (1,)), ((), ())), preferre...]
    reduce_scatter x1, waiting for transfers between devices: 10.8 us -> 2.39 us  [on_device(): lax.psum_scatter(lax.dot_general(block, w_in, (((1,), (1,)), ((), ())), p...]
    all_to_all x0 -> x1, starting transfers between devices: none -> 6.99 us  [launch_the_shelves(): lax.all_to_all(jnp.tile(page, [count_all if it == 0 else 1 for it in rang...]
    another operation x0 -> x1, local copies, waits for them, and re-layouts: none -> 6.07 us  [launch_the_shelves(): jnp.tile(page, [count_all if it == 0 else 1 for it in range(page.ndim)])]
    dot_general x1, matrix products: 11.9 us -> 17.6 us  [on_device(): lax.dot_general(hidden, grad_all, (((0,), (0,)), ((), ())), preferred_ele...]
    convert_element_type x1, other arithmetic: 13.7 us -> 19.3 us  [on_device(): pre_grad = (total * slope).astype(jnp.bfloat16)]
  transfers between devices with their start and end apart: 5 -> 5, of which waited for: 4 -> 4; matrix products, arithmetic and copies ran while one was open for 12% -> 14% of each run, Pallas kernels for 0% -> 0%
where the time goes in v1:
time: 463 us
  waiting for transfers between devices  361 us (78%)
  matrix products  46.6 us (10%)
  other arithmetic  19.3 us (4%)
  local copies, waits for them, and re-layouts  14.3 us (3%)
  between operations  13.8 us (3%)
  starting transfers between devices  7.32 us (2%)
    all_to_all x1, waiting for transfers between devices, launch_the_shelves(): lax.all_to_all(jnp.tile(page, [count_all if it == 0 else 1 for it in rang...  217 us
    psum x1, waiting for transfers between devices, on_device(): lax.psum(lax.dot_general(block, w_out, (((1,), (1,)), ((), ())), preferre...  112 us
    all_gather x1, waiting for transfers between devices, on_device(): lax.all_gather(out_grad, 'col', axis=0, tiled=True)  28.5 us
    convert_element_type x1, other arithmetic, on_device(): pre_grad = (total * slope).astype(jnp.bfloat16)  19.3 us
    dot_general x1, matrix products, on_device(): lax.dot_general(hidden, grad_all, (((0,), (0,)), ((), ())), preferred_ele...  17.6 us
    dot_general x1, matrix products, on_device(): lax.dot_general(block, w_out, (((1,), (1,)), ((), ())), preferred_element...  11.1 us
    dot_general x1, matrix products, on_device(): lax.dot_general(inputs_all, pre_grad, (((0,), (0,)), ((), ())), preferred...  10.2 us
  transfers between devices with their start and end apart: 5, of which 4 were waited for; matrix products, arithmetic and copies ran while one was open for 14% of the time, Pallas kernels for 0%

profile of v1, /device:TPU:0, one launch (start us, length us, event | category | flops | bytes accessed | tf_op | source)
XLA Modules:
  0.0 462.7 jit_solution(16991427651168239457)
XLA Ops:
  7.2 0.0 copy-start
  7.2 0.0 all-gather.3.cloned.1.call-start
  7.2 0.7 all-gather.3.cloned.1.call-update
  7.9 0.0 all-reduce.2.cloned.1.call-start
  8.0 28.5 %all-gather.3.cloned.1.call-done = bf16[2048,384]{1,0:T(8,128)(2,1)} async-done(((bf16[256,384]{1,0:T(8,128)(2,1)}), bf16[2048,384]{1,0:T(8,128)(2,1)}) %all-gather.3.cloned.1.call-update) | async-done | bytes 1572880 | tf_op jit(solution)/shard_map/all_gather | solution.py:29
  36.5 11.1 %convolution_convert_fusion = bf16[2048,3072]{1,0:T(8,128)(2,1)} fusion(bf16[2048,384]{1,0:T(8,128)(2,1)} %all-gather.3.cloned.1.call-done, bf16[3072,384]{1,0:T(8,128)(2,1)S(1)} %copy-done), kind=kOutput, calls=%fused_computation.15 | convolution fusion | flops 4838129664 | bytes 16515072 | tf_op jit(solution)/shard_map/dot_general | solution.py:33
  47.6 0.0 all-reduce.2.cloned.1.call-update
  47.6 1.1 copy-done.3
  48.7 6.1 %tile.2 = bf16[16,128,3072]{2,1,0:T(8,128)(2,1)} broadcast(bf16[128,3072]{1,0:T(8,128)(2,1)S(1)} %copy-done.3), dimensions={1,2} | broadcast | bytes 13369344 | tf_op jit(solution)/shard_map/tile | solution.py:10
  54.8 7.0 %all-to-all-start = ((bf16[16,128,3072]{2,1,0:T(8,128)(2,1)}), bf16[16,128,3072]{2,1,0:T(8,128)(2,1)}, u32[]{:S(2)}, u32[]{:S(2)}) async-start(bf16[16,128,3072]{2,1,0:T(8,128)(2,1)} %tile.2), calls=%async_computation | async-start | bytes 25165824 | tf_op jit(solution)/shard_map/all_to_all | solution.py:9
  61.8 0.0 all-gather.5.cloned.1.call-start
  61.8 0.7 all-gather.5.cloned.1.call-update
  62.5 0.2 reduce-scatter.2.cloned.1.call-start
  62.8 216.9 %all-to-all-done = bf16[16,128,3072]{2,1,0:T(8,128)(2,1)} async-done(((bf16[16,128,3072]{2,1,0:T(8,128)(2,1)}), bf16[16,128,3072]{2,1,0:T(8,128)(2,1)}, u32[]{:S(2)}, u32[]{:S(2)}) %all-to-all-start) | async-done | bytes 12582944 | tf_op jit(solution)/shard_map/all_to_all | solution.py:9
  279.7 112.1 %all-reduce.2.cloned.1.call-done = bf16[2048,3072]{1,0:T(8,128)(2,1)} async-done(((bf16[2048,3072]{1,0:T(8,128)(2,1)}), bf16[2048,3072]{1,0:T(8,128)(2,1)}) %all-reduce.2.cloned.1.call-update) | async-done | bytes 12582928 | tf_op jit(solution)/shard_map/psum | solution.py:32
  391.8 19.3 %fusion.7 = (bf16[2048,3072]{1,0:T(8,128)(2,1)S(1)}, f32[2048,3072]{1,0:T(8,128)}) fusion(bf16[2048,3072]{1,0:T(8,128)(2,1)} %all-reduce.2.cloned.1.call-done, bf16[16,128,3072]{2,1,0:T(8,128)(2,1)} %all-to-all-done), kind=kLoop, calls=%fused_computation.12 | loop fusion | flops 75497472 | bytes 62914560 | tf_op jit(solution)/shard_map/convert_element_type | solution.py:41
  411.0 4.5 copy-done.2
  415.5 7.8 %convolution_convert_fusion.2 = bf16[2048,384]{1,0:T(8,128)(2,1)} fusion(bf16[2048,3072]{1,0:T(8,128)(2,1)S(1)} %get-tuple-element.6, bf16[384,3072]{1,0:T(8,128)(2,1)S(1)} %copy-done.4), kind=kOutput, calls=%fused_computation.19 | convolution fusion | flops 4832624640 | bytes 16515072 | tf_op jit(solution)/shard_map/dot_general | solution.py:50
  423.3 0.0 reduce-scatter.2.cloned.1.call-update
  423.3 0.0 all-gather.5.cloned.1.call-done
  423.3 10.2 %fusion.14 = bf16[384,3072]{0,1:T(8,128)(2,1)S(1)} fusion(bf16[2048,3072]{1,0:T(8,128)(2,1)} %copy-done.2, bf16[2048,384]{1,0:T(8,128)(2,1)} %all-gather.5.cloned.1.call-done), kind=kOutput, calls=%fused_computation.18 | convolution fusion | flops 4833017856 | bytes 16515072 | tf_op jit(solution)/shard_map/dot_general | solution.py:45
  433.5 2.6 copy.8
  436.1 17.6 %fusion.11 = bf16[3072,384]{1,0:T(8,128)(2,1)} fusion(bf16[2048,384]{1,0:T(8,128)(2,1)} %all-gather.3.cloned.1.call-done, f32[2048,3072]{1,0:T(8,128)} %get-tuple-element.7, bf16[2048,3072]{1,0:T(8,128)(2,1)} %bitcast.1), kind=kOutput, calls=%fused_computation.16 | convolution fusion | flops 4851892224 | bytes 41680896 | tf_op jit(solution)/shard_map/dot_general | solution.py:42
  453.7 2.4 reduce-scatter.2.cloned.1.call-done
  (7 shorter events, 0.0 us)
Async XLA Ops:
  7.2 29.3 %copy-start = (bf16[3072,384]{1,0:T(8,128)(2,1)S(1)}, bf16[3072,384]{1,0:T(8,128)(2,1)}, u32[]{:S(2)}) copy-start(bf16[3072,384]{1,0:T(8,128)(2,1)} %param.9) | copy-start | bytes 7077892
  7.2 29.3 %all-gather.3.cloned.1.call-start = ((), (), s32[]{:S(2)}) async-start(), calls=%async_computation.2 | async-start | bytes 1769472 | tf_op jit(solution)/shard_map/all_gather | solution.py:29
  7.9 383.9 %all-reduce.2.cloned.1.call-start = ((), (), s32[]{:S(2)}) async-start(), calls=%async_computation.3 | async-start | bytes 25165824 | tf_op jit(solution)/shard_map/psum | solution.py:32
  47.6 1.1 copy-start.3
  54.8 224.9 %all-to-all-start = ((bf16[16,128,3072]{2,1,0:T(8,128)(2,1)}), bf16[16,128,3072]{2,1,0:T(8,128)(2,1)}, u32[]{:S(2)}, u32[]{:S(2)}) async-start(bf16[16,128,3072]{2,1,0:T(8,128)(2,1)} %tile.2), calls=%async_computation | async-start | bytes 25165824 | tf_op jit(solution)/shard_map/all_to_all | solution.py:9
  61.8 361.5 %all-gather.5.cloned.1.call-start = ((), (), s32[]{:S(2)}) async-start(), calls=%async_computation.5 | async-start | bytes 1769472 | tf_op jit(solution)/shard_map/all_gather | solution.py:28
  62.5 353.0 %copy-start.4 = (bf16[384,3072]{1,0:T(8,128)(2,1)S(1)}, bf16[384,3072]{1,0:T(8,128)(2,1)}, u32[]{:S(2)}) copy-start(bf16[384,3072]{1,0:T(8,128)(2,1)} %param.8) | copy-start | bytes 7077892
  62.5 393.6 %reduce-scatter.2.cloned.1.call-start = ((), (), s32[]{:S(2)}) async-start(), calls=%async_computation.4 | async-start | bytes 1769472 | tf_op jit(solution)/shard_map/reduce_scatter | solution.py:49
  411.0 4.5 copy-start.2
  436.1 20.0 %copy-start.1 = (bf16[3072,384]{1,0:T(8,128)(2,1)S(1)}, bf16[3072,384]{1,0:T(8,128)(2,1)}, u32[]{:S(2)}) copy-start(bf16[3072,384]{1,0:T(8,128)(2,1)} %param.9) | copy-start | bytes 7077892
Sparse Core Ops, SparseCore 0:
  9.7 26.7 all-gather.2
  47.7 344.0 all-reduce.1
  393.5 23.9 all-gather.4
  423.4 32.6 reduce-scatter.1
